TPU v7x, 128 devices: a whole 4x4x4 slice. The times are simulated.
128 devices in a mesh: req: 16 (over y, z), mp: 8 (over x, core).
Axes of the slice: x: 4, y: 4, z: 4, core: 2. Of those that a mesh axis runs over, the one named last changes fastest.
Arguments:
- hidden_in: bfloat16 [16384, 2048], P('req', 'mp'), may hold values from -6 to 6
- w_qkv: bfloat16 [3, 2048, 2048], P(None, 'req', 'mp'), may hold values from -0.125 to 0.125
- w_out: bfloat16 [2048, 2048], P('mp', 'req'), may hold values from -0.125 to 0.125
- attn_gain: bfloat16 [2048], replicated, may hold values from 0.099609375 to 1.8984375
- mlp_gain: bfloat16 [2048], replicated, may hold values from 0.099609375 to 1.8984375
- w_gate: bfloat16 [2048, 8192], P('req', 'mp'), may hold values from -0.125 to 0.125
- w_up: bfloat16 [2048, 8192], P('req', 'mp'), may hold values from -0.125 to 0.125
- w_down: bfloat16 [8192, 2048], P('mp', 'req'), may hold values from -0.0625 to 0.0625
- k_cache: bfloat16 [16, 4096, 2048], P('req', None, 'mp'), may hold values from -363 to 363
- v_cache: bfloat16 [16, 4096, 2048], P('req', None, 'mp'), may hold values from -6 to 6
- cache_len: int32 [16], P('req'), may hold values from 256 to 4096, as said below
Outputs:
- hidden_out: bfloat16 [16384, 2048], P('req', 'mp')
- new_keys: bfloat16 [16384, 2048], P('req', 'mp')
- new_values: bfloat16 [16384, 2048], P('req', 'mp')
Inputs may be any that keep to these rules, and one draw needn't show every extreme that they name: Each request uses its first cache_len slots; later slots hold unused data. Some request's cache is full in every draw.
All inputs are finite; a program needn't handle non-finite values.
Results may differ from a plain program's by a relative error of at most 0.02.
Values may be sent and summed in bfloat16 or wider, within the bound.
No kernel may reach another device: no remote copies, remote signals or barrier semaphores. Data moves between devices by JAX's collectives and lax.ppermute only.
A program may use at most 128 MiB of HBM per device.

v0:
```python
import jax
import jax.numpy as jnp
from jax import lax
from jax.sharding import PartitionSpec as P

HD = 64
THETA = 130000.0
EPSILON = 1e-05
NEG_FILL = -1e30


def rms_scale(rows, gain):
    values = rows.astype(jnp.float32)
    meansq = jnp.mean(values * values, axis=-1, keepdims=True)
    return (values * lax.rsqrt(meansq + EPSILON) * gain.astype(jnp.float32)).astype(jnp.bfloat16)


def rotate(tensor, positions):
    half = tensor.shape[-1] // 2
    freq = THETA ** (-(jnp.arange(half, dtype=jnp.float32) * 2.0 / tensor.shape[-1]))
    angle = positions[:, None, None] * freq[None, None, :]
    cosine = jnp.cos(angle)
    sine = jnp.sin(angle)
    first = tensor[..., :half]
    second = tensor[..., half:]
    return jnp.concatenate(
        [first * cosine - second * sine, second * cosine + first * sine], axis=-1
    )


def gather_packed(blocks, axes, axis_name):
    count = lax.axis_size(axis_name)
    lane = 128
    joined = jnp.concatenate([block.reshape(-1, lane) for block in blocks], axis=0)
    gathered = lax.all_gather(joined, axis_name, axis=0, tiled=False)
    outs = []
    offset = 0
    for block, axis in zip(blocks, axes):
        rows = block.size // lane
        piece = gathered[:, offset : offset + rows].reshape((count,) + block.shape)
        piece = jnp.moveaxis(piece, 0, axis)
        shape = list(block.shape)
        shape[axis] *= count
        outs.append(piece.reshape(shape))
        offset += rows
    return outs


def absorb(carry, queries, keys, values, valid):
    top, total, accum = carry
    scores = jnp.einsum("qhd,khd->hqk", queries, keys, preferred_element_type=jnp.float32) * HD ** (
        -0.5
    )
    scores = jnp.where(valid[None], scores, NEG_FILL)
    new_top = jnp.maximum(top, jnp.max(scores, axis=-1, keepdims=True))
    factor = jnp.exp(top - new_top)
    probs = jnp.where(valid[None], jnp.exp(scores - new_top), 0.0)
    total = total * factor + jnp.sum(probs, axis=-1, keepdims=True)
    accum = accum * factor + jnp.einsum(
        "hqk,khd->hqd", probs.astype(jnp.bfloat16), values, preferred_element_type=jnp.float32
    )
    return (new_top, total, accum)


def on_device(
    hidden_in, w_qkv, w_out, attn_gain, mlp_gain, w_gate, w_up, w_down, k_cache, v_cache, cache_len
):
    new_count = hidden_in.shape[0]
    w_qkv_full = lax.all_gather(w_qkv, "req", axis=1, tiled=True)
    w_gate_full, w_up_full, w_down_full, w_out_full = gather_packed(
        [w_gate, w_up, w_down, w_out], [0, 0, 1, 1], "req"
    )
    width = w_qkv.shape[2]
    heads_local = width // HD
    slots = k_cache.shape[1]
    full_rows = lax.all_gather(hidden_in, "mp", axis=1, tiled=True)
    normed = rms_scale(full_rows, attn_gain)
    columns = normed
    projected = jnp.einsum("nd,kdw->knw", columns, w_qkv_full, preferred_element_type=jnp.float32)
    length = cache_len[0]
    positions = (length + jnp.arange(new_count, dtype=jnp.int32)).astype(jnp.float32)
    queries = rotate(projected[0].reshape(new_count, heads_local, HD), positions).astype(
        jnp.bfloat16
    )
    fresh_keys = rotate(projected[1].reshape(new_count, heads_local, HD), positions).astype(
        jnp.bfloat16
    )
    fresh_values = projected[2].astype(jnp.bfloat16).reshape(new_count, heads_local, HD)
    rows = jnp.arange(new_count, dtype=jnp.int32)
    causal = rows[:, None] >= rows[None, :]
    start_carry = (
        jnp.full((heads_local, new_count, 1), NEG_FILL, jnp.float32),
        jnp.zeros((heads_local, new_count, 1), jnp.float32),
        jnp.zeros((heads_local, new_count, HD), jnp.float32),
    )
    carry = absorb(start_carry, queries, fresh_keys, fresh_values, causal)
    cache_keys = k_cache[0].reshape(slots, heads_local, HD)
    cache_values = v_cache[0].reshape(slots, heads_local, HD)
    block = min(slots, 512)
    count = (length + block - 1) // block

    def step_block(index, state):
        begin = index * block
        keys = lax.dynamic_slice_in_dim(cache_keys, begin, block, 0)
        values = lax.dynamic_slice_in_dim(cache_values, begin, block, 0)
        valid = (begin + jnp.arange(block, dtype=jnp.int32) < length)[None, :]
        return absorb(state, queries, keys, values, valid)

    top, total, accum = lax.fori_loop(0, count, step_block, carry)
    attn = (accum / total).transpose(1, 0, 2).reshape(new_count, width).astype(jnp.bfloat16)
    partial_value = jnp.dot(attn, w_out_full, preferred_element_type=jnp.float32)
    summed = lax.psum(partial_value.astype(jnp.bfloat16), "mp").astype(jnp.float32)
    mid_full = (full_rows.astype(jnp.float32) + summed).astype(jnp.bfloat16)
    own = hidden_in.shape[1]
    mid_local = lax.dynamic_slice_in_dim(mid_full, lax.axis_index("mp") * own, own, axis=1)
    normed2 = rms_scale(mid_full, mlp_gain)
    columns = normed2
    gate = jnp.dot(columns, w_gate_full, preferred_element_type=jnp.float32)
    upper = jnp.dot(columns, w_up_full, preferred_element_type=jnp.float32)
    units = (jax.nn.silu(gate) * upper).astype(jnp.bfloat16)
    terms = jnp.dot(units, w_down_full, preferred_element_type=jnp.float32)
    reduced = lax.psum_scatter(
        terms.astype(jnp.bfloat16), "mp", scatter_dimension=1, tiled=True
    ).astype(jnp.float32)
    hidden_out = (mid_local.astype(jnp.float32) + reduced).astype(jnp.bfloat16)
    return (
        hidden_out,
        fresh_keys.reshape(new_count, width),
        fresh_values.reshape(new_count, width),
    )


def solution(mesh):
    return jax.shard_map(
        on_device,
        mesh=mesh,
        in_specs=(
            P("req", "mp"),
            P(None, "req", "mp"),
            P("mp", "req"),
            P(),
            P(),
            P("req", "mp"),
            P("req", "mp"),
            P("mp", "req"),
            P("req", None, "mp"),
            P("req", None, "mp"),
            P("req"),
        ),
        out_specs=(P("req", "mp"), P("req", "mp"), P("req", "mp")),
        check_vma=False,
    )
```

profile of v0, /device:TPU:0, one launch (start us, length us, event | category | flops | bytes accessed | tf_op | source)
XLA Modules:
  0.0 353.1 jit_solution(15132475671423839923)
XLA Ops:
  14.6 2.9 copy.31
  17.6 4.1 %copy.32 = bf16[1,4096,256]{1,2,0:T(8,128)(2,1)} copy(bf16[1,4096,256]{2,1,0:T(8,128)(2,1)} %param.22) | data formatting | bytes 4194304 | tf_op args[9]
  23.5 24.7 %all-gather.5.cloned.1.call-done = bf16[1024,2048]{1,0:T(8,128)(2,1)} async-done(((bf16[1024,256]{1,0:T(8,128)(2,1)}), bf16[1024,2048]{1,0:T(8,128)(2,1)}) %all-gather.5.cloned.1.call-update) | async-done | bytes 4194320 | tf_op jit(solution)/shard_map/all_gather | solution.py:76
  48.2 3.1 fusion.26
  51.3 53.4 %all-gather.7.cloned.1.call-done = bf16[3,2048,256]{1,2,0:T(8,128)(2,1)} async-done(((bf16[3,128,256]{1,2,0:T(8,128)(2,1)}), bf16[3,2048,256]{1,2,0:T(8,128)(2,1)}) %all-gather.7.cloned.1.call-update) | async-done | bytes 3145744 | tf_op jit(solution)/shard_map/all_gather | solution.py:69
  104.7 6.6 %fusion.38 = f32[3,1024,256]{1,2,0:T(8,128)S(1)} fusion(bf16[3,2048,256]{1,2,0:T(8,128)(2,1)} %all-gather.7.cloned.1.call-done, bf16[1024,2048]{1,0:T(8,128)(2,1)} %all-gather.5.cloned.1.call-done, f32[2048]{0:T(1024)S(1)} %convert_element_type.84, f32[1024]{0:T(1024)S(1)} %add_rsqrt_fusion.1), kind=kOutput, calls=%fused_computation.52 | convolution fusion | flops 3229614080 | bytes 10498048 | tf_op jit(solution)/shard_map/nd,kdw->knw/dot_general | solution.py:79
  113.8 3.0 fusion.20
  116.8 4.2 %fusion.22 = f32[4,1024]{1,0:T(4,128)S(1)} fusion(f32[4,1024,1024]{1,2,0:T(8,128)S(1)} %get-tuple-element.102, f32[4,1024]{1,0:T(4,128)S(1)} %get-tuple-element.98, pred[1024,1024]{0,1:T(8,128)(4,1)S(1)} %copy-done.1), kind=kLoop, calls=%fused_computation.31 | loop fusion | flops 20967424 | bytes 17858560 | tf_op jit(solution)/shard_map/reduce_sum | solution.py:58
  121.1 5.9 %fusion.41 = f32[4,1024,64]{1,2,0:T(8,128)} fusion(bf16[1024,4,64]{0,2,1:T(8,128)(2,1)S(1)} %bitcast.91, f32[4,1024,1024]{1,2,0:T(8,128)S(1)} %get-tuple-element.102, f32[4,1024]{1,0:T(4,128)S(1)} %get-tuple-element.98, pred[1024,1024]{0,1:T(8,128)(4,1)S(1)} %copy-done.1, f32[4,1024]{1,0:T(4,128)S(1)} %get-tuple-element.96), kind=kOutput, calls=%fused_computation.53 | convolution fusion | flops 558104576 | bytes 19431424 | tf_op jit(solution)/shard_map/hqk,khd->hqd/dot_general | solution.py:59
  127.0 8.0 %while.14 = (s32[]{:T(128)}, f32[4,1024,1]{1,0,2:T(4,128)S(1)}, f32[4,1024,1]{1,0,2:T(4,128)S(1)}, f32[4,1024,64]{1,2,0:T(8,128)}, s32[]{:T(128)}, /*index=5*/s3...) while((s32[]{:T(128)}, f32[4,1024,1]{1,0,2:T(4,128)S(1)}, ...), condition=%wide.region_6.7_spmd, body=%wide.region_3.6_spmd.sunk | while | flops 564671488 | bytes 36965104 | solution.py:109
  129.3 3.1 fusion.77
  132.4 2.5 fusion.76
  136.3 65.2 %all-gather.9.cloned.1.call-done = bf16[53248,128]{1,0:T(8,128)(2,1)} async-done(((bf16[3328,128]{1,0:T(8,128)(2,1)}), bf16[53248,128]{1,0:T(8,128)(2,1)}) %all-gather.9.cloned.1.call-update) | async-done | bytes 13631504 | tf_op jit(solution)/shard_map/all_gather | solution.py:35
  203.4 3.3 convolution_convert_fusion
  207.4 9.1 %fusion.56 = (bf16[16,1024,128]{2,1,0:T(8,128)(2,1)}, bf16[1024,16,128]{2,0,1:T(8,128)(2,1)}, bf16[16,1024,128]{2,1,0:T(8,128)(2,1)}) fusion(bf16[16,3328,128]{2,1,0:T(8,128)(2,1)} %bitcast.79), kind=kLoop, calls=%fused_computation.81 | loop fusion | bytes 25165824 | tf_op jit(solution)/shard_map/slice | solution.py:40
  216.5 7.4 %reshape_reshape.6 = bf16[2048,1024]{1,0:T(8,128)(2,1)} reshape(bf16[16,1024,128]{2,1,0:T(8,128)(2,1)} %get-tuple-element.89) | data formatting | bytes 8388608 | tf_op jit(solution)/shard_map/reshape;reshape | solution.py:44
  223.9 6.4 %copy.34 = bf16[1024,16,128]{0,2,1:T(8,128)(2,1)} copy(bf16[1024,16,128]{2,0,1:T(8,128)(2,1)} %get-tuple-element.88) | data formatting | bytes 8388608 | tf_op jit(solution)/shard_map/transpose | solution.py:41
  230.4 7.4 %reshape_reshape.7 = bf16[2048,1024]{1,0:T(8,128)(2,1)} reshape(bf16[16,1024,128]{2,1,0:T(8,128)(2,1)} %get-tuple-element.87) | data formatting | bytes 8388608 | tf_op jit(solution)/shard_map/reshape;reshape | solution.py:44
  237.8 41.3 %all-reduce.2.cloned.1.call-done = bf16[1024,2048]{1,0:T(8,128)(2,1)} async-done(((bf16[1024,2048]{1,0:T(8,128)(2,1)}), bf16[1024,2048]{1,0:T(8,128)(2,1)}) %all-reduce.2.cloned.1.call-update) | async-done | bytes 4194320 | tf_op jit(solution)/shard_map/psum | solution.py:112
  279.0 5.6 %fusion.23 = (f32[1024]{0:T(1024)S(1)}, bf16[1024,2048]{1,0:T(8,128)(2,1)S(1)}) fusion(bf16[1024,2048]{1,0:T(8,128)(2,1)} %all-reduce.2.cloned.1.call-done, bf16[1024,2048]{1,0:T(8,128)(2,1)} %all-gather.5.cloned.1.call-done), kind=kLoop, calls=%fused_computation.34 | loop fusion | flops 14679040 | bytes 12587008 | tf_op jit(solution)/shard_map/reduce_sum | solution.py:14
  284.7 6.3 %fusion.45 = f32[1024,1024]{1,0:T(8,128)} fusion(bf16[2048,1024]{1,0:T(8,128)(2,1)S(1)} %copy-done.2, bf16[1024,2048]{1,0:T(8,128)(2,1)S(1)} %get-tuple-element.84, f32[2048]{0:T(1024)S(1)} %convert_element_type.99, f32[1024]{0:T(1024)S(1)} %add_rsqrt_fusion), kind=kOutput, calls=%fused_computation.54 | convolution fusion | flops 4303355904 | bytes 12595200 | tf_op jit(solution)/shard_map/dot_general | solution.py:118
  291.0 15.4 %convolution_convert_fusion.1 = bf16[1024,2048]{1,0:T(8,128)(2,1)} fusion(bf16[1024,2048]{0,1:T(8,128)(2,1)} %bitcast.84, f32[1024,1024]{1,0:T(8,128)} %fusion.45, bf16[2048,1024]{1,0:T(8,128)(2,1)} %reshape_reshape.7, bf16[1024,2048]{1,0:T(8,128)(2,1)} %copy-done, f32[2048]{0:T(1024)S(1)} %convert_element_type.99, f32[1024]{0:T(1024)S(1)} %add_rsqrt_fusion), kind=kOutput, calls=%fused_computation.51 | convolution fusion | flops 8606711808 | bytes 20983808 | tf_op jit(solution)/shard_map/dot_general | solution.py:121
  309.7 34.8 %reduce-scatter.2.cloned.1.call-done = bf16[1024,256]{1,0:T(8,128)(2,1)} async-done(((bf16[1024,2048]{1,0:T(8,128)(2,1)}), bf16[1024,256]{1,0:T(8,128)(2,1)}) %reduce-scatter.2.cloned.1.call-update) | async-done | bytes 524304 | tf_op jit(solution)/shard_map/reduce_scatter | solution.py:122
  344.5 2.1 add_convert_fusion
  (59 shorter events, 20.5 us)
Async XLA Ops:
  7.2 7.4 %copy-start.7 = (bf16[2048]{0:T(1024)(128)(2,1)S(1)}, bf16[2048]{0:T(1024)(128)(2,1)}, u32[]{:S(2)}) copy-start(bf16[2048]{0:T(1024)(128)(2,1)} %param.16) | copy-start | bytes 12292
  7.2 41.0 %all-gather.5.cloned.1.call-start = ((), (), s32[]{:S(2)}) async-start(), calls=%async_computation.1 | async-start | bytes 4718592 | tf_op jit(solution)/shard_map/all_gather | solution.py:76
  7.9 96.8 %all-gather.7.cloned.1.call-start = ((), (), s32[]{:S(2)}) async-start(), calls=%async_computation.2 | async-start | bytes 3342336 | tf_op jit(solution)/shard_map/all_gather | solution.py:69
  9.7 191.8 %all-gather.9.cloned.1.call-start = ((), (), s32[]{:S(2)}) async-start(), calls=%async_computation.5 | async-start | bytes 14483456 | tf_op jit(solution)/shard_map/all_gather | solution.py:35
  13.9 265.1 %all-reduce.2.cloned.1.call-start = ((), (), s32[]{:S(2)}) async-start(), calls=%async_computation.3 | async-start | bytes 8388608 | tf_op jit(solution)/shard_map/psum | solution.py:112
  111.3 1.8 copy-start.3
  112.3 1.5 copy-start.1
  116.8 4.2 %copy-start.6 = (bf16[1,1024,256]{1,2,0:T(8,128)(2,1)S(1)}, bf16[1,1024,256]{1,2,0:T(8,128)(2,1)}, u32[]{:S(2)}) copy-start(bf16[1,1024,256]{1,2,0:T(8,128)(2,1)} %slice.66) | copy-start | bytes 1572868
  127.7 1.6 copy-start.4
  132.4 2.6 copy-start.5
  206.7 0.7 copy-start.8
  206.7 137.7 %reduce-scatter.2.cloned.1.call-start = ((), (), s32[]{:S(2)}) async-start(), calls=%async_computation.4 | async-start | bytes 4718592 | tf_op jit(solution)/shard_map/reduce_scatter | solution.py:122
  279.0 5.6 %copy-start.2 = (bf16[2048,1024]{1,0:T(8,128)(2,1)S(1)}, bf16[2048,1024]{1,0:T(8,128)(2,1)}, u32[]{:S(2)}) copy-start(bf16[2048,1024]{1,0:T(8,128)(2,1)} %reshape_reshape.6) | copy-start | bytes 12582916
  284.6 6.4 %copy-start = (bf16[1024,2048]{1,0:T(8,128)(2,1)}, bf16[1024,2048]{1,0:T(8,128)(2,1)S(1)}, u32[]{:S(2)}) copy-start(bf16[1024,2048]{1,0:T(8,128)(2,1)S(1)} %get-tuple-element.84) | copy-start | bytes 12582916
Sparse Core Ops, SparseCore 0:
  9.7 38.4 all-gather.4
  50.9 53.7 all-gather.6
  106.9 94.6 all-gather.8
  206.9 72.1 all-reduce.1
  306.5 37.9 reduce-scatter.1
where the time goes:
time: 354 us; the launch traced here: 353 us
  waiting for transfers between devices  220 us (62%)
  local copies, waits for them, and re-layouts  48.9 us (14%)
  matrix products  45.3 us (13%)
  other arithmetic  23.8 us (7%)
  between operations  14.7 us (4%)
    all_gather x1, waiting for transfers between devices, gather_packed(): gathered = lax.all_gather(joined, axis_name, axis=0, tiled=False)  65.2 us
    all_gather x1, waiting for transfers between devices, on_device(): w_qkv_full = lax.all_gather(w_qkv, 'req', axis=1, tiled=True)  53.4 us
    psum x1, waiting for transfers between devices, on_device(): lax.psum(partial_value.astype(jnp.bfloat16), 'mp').astype(jnp.float32)  41.3 us
    reduce_scatter x1, waiting for transfers between devices, on_device(): lax.psum_scatter(terms.astype(jnp.bfloat16), 'mp', scatter_dimension=1, t...  34.8 us
    all_gather x1, waiting for transfers between devices, on_device(): full_rows = lax.all_gather(hidden_in, 'mp', axis=1, tiled=True)  24.7 us
    dot_general x1, matrix products, on_device(): terms = jnp.dot(units, w_down_full, preferred_element_type=jnp.float32)  15.4 us
    another operation x2, local copies, waits for them, and re-layouts, gather_packed(): outs.append(piece.reshape(shape))  14.8 us
    unnamed x19, local copies, waits for them, and re-layouts  12.2 us
  transfers between devices with their start and end apart: 5, of which 5 were waited for; matrix products, arithmetic and copies ran while one was open for 23% of the time, Pallas kernels for 0%

commit v1 on v0

--- a/solution.py
+++ b/solution.py
@@ -1,12 +1,21 @@
+import functools
 import jax
 import jax.numpy as jnp
 from jax import lax
 from jax.sharding import PartitionSpec as P
+from jax.lax import all_gather
 
 HD = 64
 THETA = 130000.0
 EPSILON = 1e-05
 NEG_FILL = -1e30
+
+
+def sheet_show(packet, a_name):
+    return all_gather(packet, axis_name=a_name).sum(axis=0)
+
+
+process_trails_here = functools.partial(sheet_show, a_name="mp")
 
 
 def rms_scale(rows, gain):
@@ -109,7 +118,7 @@
     top, total, accum = lax.fori_loop(0, count, step_block, carry)
     attn = (accum / total).transpose(1, 0, 2).reshape(new_count, width).astype(jnp.bfloat16)
     partial_value = jnp.dot(attn, w_out_full, preferred_element_type=jnp.float32)
-    summed = lax.psum(partial_value.astype(jnp.bfloat16), "mp").astype(jnp.float32)
+    summed = process_trails_here(partial_value.astype(jnp.bfloat16)).astype(jnp.float32)
     mid_full = (full_rows.astype(jnp.float32) + summed).astype(jnp.bfloat16)
     own = hidden_in.shape[1]
     mid_local = lax.dynamic_slice_in_dim(mid_full, lax.axis_index("mp") * own, own, axis=1)

time: 354 us -> 453 us (1.28)
  waiting for transfers between devices: 220 us -> 302 us
  other arithmetic: 23.8 us -> 38 us
    all_gather x0 -> x1, waiting for transfers between devices: none -> 124 us  [sheet_show(): return all_gather(packet, axis_name=a_name).sum(axis=0)]
    psum x1 -> x0, waiting for transfers between devices: 41.3 us -> none  [on_device(): lax.psum(partial_value.astype(jnp.bfloat16), 'mp').astype(jnp.float32)]
    reduce_sum x0 -> x1, other arithmetic: none -> 14.2 us  [sheet_show(): return all_gather(packet, axis_name=a_name).sum(axis=0)]
  transfers between devices with their start and end apart: 5 -> 5, of which waited for: 5 -> 5; matrix products, arithmetic and copies ran while one was open for 23% -> 18% of each run, Pallas kernels for 0% -> 0%
where the time goes in v1:
time: 453 us; the launch traced here: 452 us
  waiting for transfers between devices  302 us (67%)
  local copies, waits for them, and re-layouts  50.7 us (11%)
  matrix products  45.4 us (10%)
  other arithmetic  38 us (8%)
  between operations  14.7 us (3%)
    all_gather x1, waiting for transfers between devices, sheet_show(): return all_gather(packet, axis_name=a_name).sum(axis=0)  124 us
    all_gather x1, waiting for transfers between devices, gather_packed(): gathered = lax.all_gather(joined, axis_name, axis=0, tiled=False)  64.2 us
    all_gather x1, waiting for transfers between devices, on_device(): w_qkv_full = lax.all_gather(w_qkv, 'req', axis=1, tiled=True)  53.4 us
    reduce_scatter x1, waiting for transfers between devices, on_device(): lax.psum_scatter(terms.astype(jnp.bfloat16), 'mp', scatter_dimension=1, t...  35.6 us
    all_gather x1, waiting for transfers between devices, on_device(): full_rows = lax.all_gather(hidden_in, 'mp', axis=1, tiled=True)  24.7 us
    dot_general x1, matrix products, on_device(): terms = jnp.dot(units, w_down_full, preferred_element_type=jnp.float32)  15.4 us
    another operation x2, local copies, waits for them, and re-layouts, gather_packed(): outs.append(piece.reshape(shape))  15.1 us
    reduce_sum x1, other arithmetic, sheet_show(): return all_gather(packet, axis_name=a_name).sum(axis=0)  14.2 us
  transfers between devices with their start and end apart: 5, of which 5 were waited for; matrix products, arithmetic and copies ran while one was open for 18% of the time, Pallas kernels for 0%

profile of v1, /device:TPU:0, one launch (start us, length us, event | category | flops | bytes accessed | tf_op | source)
XLA Modules:
  0.0 451.6 jit_solution(3264592087518505199)
XLA Ops:
  14.6 2.9 copy.31
  17.5 4.1 copy.32
  23.5 24.7 %all-gather.7.cloned.1.call-done = bf16[1024,2048]{1,0:T(8,128)(2,1)} async-done(((bf16[1024,256]{1,0:T(8,128)(2,1)}), bf16[1024,2048]{1,0:T(8,128)(2,1)}) %all-gather.7.cloned.1.call-update) | async-done | bytes 4194320 | tf_op jit(solution)/shard_map/all_gather | solution.py:85
  48.2 3.1 fusion.26
  51.3 53.4 %all-gather.9.cloned.1.call-done = bf16[3,2048,256]{1,2,0:T(8,128)(2,1)} async-done(((bf16[3,128,256]{1,2,0:T(8,128)(2,1)}), bf16[3,2048,256]{1,2,0:T(8,128)(2,1)}) %all-gather.9.cloned.1.call-update) | async-done | bytes 3145744 | tf_op jit(solution)/shard_map/all_gather | solution.py:78
  104.7 6.6 %fusion.38 = f32[3,1024,256]{1,2,0:T(8,128)S(1)} fusion(bf16[3,2048,256]{1,2,0:T(8,128)(2,1)} %all-gather.9.cloned.1.call-done, bf16[1024,2048]{1,0:T(8,128)(2,1)} %all-gather.7.cloned.1.call-done, f32[2048]{0:T(1024)S(1)} %convert_element_type.86, f32[1024]{0:T(1024)S(1)} %add_rsqrt_fusion.1), kind=kOutput, calls=%fused_computation.52 | convolution fusion | flops 3229614080 | bytes 10498048 | tf_op jit(solution)/shard_map/nd,kdw->knw/dot_general | solution.py:88
  113.8 3.0 fusion.20
  116.8 4.2 fusion.22
  121.1 6.0 %fusion.41 = f32[4,1024,64]{1,2,0:T(8,128)} fusion(bf16[1024,4,64]{0,2,1:T(8,128)(2,1)S(1)} %bitcast.93, f32[4,1024,1024]{1,2,0:T(8,128)S(1)} %get-tuple-element.102, f32[4,1024]{1,0:T(4,128)S(1)} %get-tuple-element.98, pred[1024,1024]{0,1:T(8,128)(4,1)S(1)} %copy-done.1, f32[4,1024]{1,0:T(4,128)S(1)} %get-tuple-element.96), kind=kOutput, calls=%fused_computation.53 | convolution fusion | flops 558104576 | bytes 19431424 | tf_op jit(solution)/shard_map/hqk,khd->hqd/dot_general | solution.py:68
  127.1 8.9 %while.14 = (s32[]{:T(128)}, f32[4,1024,1]{1,0,2:T(4,128)S(1)}, f32[4,1024,1]{1,0,2:T(4,128)S(1)}, f32[4,1024,64]{1,2,0:T(8,128)}, s32[]{:T(128)}, /*index=5*/s3...) while((s32[]{:T(128)}, f32[4,1024,1]{1,0,2:T(4,128)S(1)}, ...), condition=%wide.region_6.7_spmd, body=%wide.region_3.6_spmd.sunk | while | flops 564671488 | bytes 36965104 | solution.py:118
  129.4 2.5 fusion.76
  131.9 3.1 fusion.77
  137.4 64.2 %all-gather.11.cloned.1.call-done = bf16[53248,128]{1,0:T(8,128)(2,1)} async-done(((bf16[3328,128]{1,0:T(8,128)(2,1)}), bf16[53248,128]{1,0:T(8,128)(2,1)}) %all-gather.11.cloned.1.call-update) | async-done | bytes 13631504 | tf_op jit(solution)/shard_map/all_gather | solution.py:44
  203.4 3.4 convolution_convert_fusion
  207.4 9.4 %fusion.56 = (bf16[16,1024,128]{2,1,0:T(8,128)(2,1)}, bf16[1024,16,128]{2,0,1:T(8,128)(2,1)}, bf16[16,1024,128]{2,1,0:T(8,128)(2,1)}) fusion(bf16[16,3328,128]{2,1,0:T(8,128)(2,1)} %bitcast.81), kind=kLoop, calls=%fused_computation.81 | loop fusion | bytes 25165824 | tf_op jit(solution)/shard_map/slice | solution.py:49
  216.8 7.7 %reshape_reshape.7 = bf16[2048,1024]{1,0:T(8,128)(2,1)} reshape(bf16[16,1024,128]{2,1,0:T(8,128)(2,1)} %get-tuple-element.87) | data formatting | bytes 8388608 | tf_op jit(solution)/shard_map/reshape;reshape | solution.py:53
  224.5 6.7 %copy.34 = bf16[1024,16,128]{0,2,1:T(8,128)(2,1)} copy(bf16[1024,16,128]{2,0,1:T(8,128)(2,1)} %get-tuple-element.88) | data formatting | bytes 8388608 | tf_op jit(solution)/shard_map/transpose | solution.py:50
  231.2 7.4 %reshape_reshape.6 = bf16[2048,1024]{1,0:T(8,128)(2,1)} reshape(bf16[16,1024,128]{2,1,0:T(8,128)(2,1)} %get-tuple-element.89) | data formatting | bytes 8388608 | tf_op jit(solution)/shard_map/reshape;reshape | solution.py:53
  238.6 123.8 %all-gather.13.cloned.1.call-done = bf16[8192,2048]{1,0:T(8,128)(2,1)} async-done(((bf16[1024,2048]{1,0:T(8,128)(2,1)}), bf16[8192,2048]{1,0:T(8,128)(2,1)}) %all-gather.13.cloned.1.call-update) | async-done | bytes 33554448 | tf_op jit(solution)/shard_map/all_gather | solution.py:15
  362.4 14.2 %reduce_sum.53 = bf16[1024,2048]{1,0:T(8,128)(2,1)} reduce(bf16[8,1024,2048]{2,1,0:T(8,128)(2,1)} %bitcast.79, bf16[]{:T(256)} %constant.68.clone.1), dimensions={0}, to_apply=%region_7.8 | reduce | flops 14680064 | bytes 37748736 | tf_op jit(solution)/shard_map/reduce_sum | solution.py:15
  376.7 5.6 %fusion.23 = (f32[1024]{0:T(1024)S(1)}, bf16[1024,2048]{1,0:T(8,128)(2,1)S(1)}) fusion(bf16[1024,2048]{1,0:T(8,128)(2,1)} %reduce_sum.53, bf16[1024,2048]{1,0:T(8,128)(2,1)} %all-gather.7.cloned.1.call-done), kind=kLoop, calls=%fused_computation.34 | loop fusion | flops 14679040 | bytes 12587008 | tf_op jit(solution)/shard_map/reduce_sum | solution.py:23
  382.3 6.3 %fusion.45 = f32[1024,1024]{1,0:T(8,128)} fusion(bf16[2048,1024]{1,0:T(8,128)(2,1)S(1)} %copy-done.2, bf16[1024,2048]{1,0:T(8,128)(2,1)S(1)} %get-tuple-element.84, f32[2048]{0:T(1024)S(1)} %convert_element_type.101, f32[1024]{0:T(1024)S(1)} %add_rsqrt_fusion), kind=kOutput, calls=%fused_computation.54 | convolution fusion | flops 4303355904 | bytes 12595200 | tf_op jit(solution)/shard_map/dot_general | solution.py:127
  388.6 15.4 %convolution_convert_fusion.1 = bf16[1024,2048]{1,0:T(8,128)(2,1)} fusion(bf16[1024,2048]{0,1:T(8,128)(2,1)} %bitcast.86, f32[1024,1024]{1,0:T(8,128)} %fusion.45, bf16[2048,1024]{1,0:T(8,128)(2,1)} %reshape_reshape.7, bf16[1024,2048]{1,0:T(8,128)(2,1)} %copy-done, f32[2048]{0:T(1024)S(1)} %convert_element_type.101, f32[1024]{0:T(1024)S(1)} %add_rsqrt_fusion), kind=kOutput, calls=%fused_computation.51 | convolution fusion | flops 8606711808 | bytes 20983808 | tf_op jit(solution)/shard_map/dot_general | solution.py:130
  407.4 35.6 %reduce-scatter.2.cloned.1.call-done = bf16[1024,256]{1,0:T(8,128)(2,1)} async-done(((bf16[1024,2048]{1,0:T(8,128)(2,1)}), bf16[1024,256]{1,0:T(8,128)(2,1)}) %reduce-scatter.2.cloned.1.call-update) | async-done | bytes 524304 | tf_op jit(solution)/shard_map/reduce_scatter | solution.py:131
  (60 shorter events, 23.6 us)
Async XLA Ops:
  7.2 7.4 %copy-start.7 = (bf16[2048]{0:T(1024)(128)(2,1)S(1)}, bf16[2048]{0:T(1024)(128)(2,1)}, u32[]{:S(2)}) copy-start(bf16[2048]{0:T(1024)(128)(2,1)} %param.16) | copy-start | bytes 12292
  7.2 41.0 %all-gather.7.cloned.1.call-start = ((), (), s32[]{:S(2)}) async-start(), calls=%async_computation.1 | async-start | bytes 4718592 | tf_op jit(solution)/shard_map/all_gather | solution.py:85
  7.9 96.8 %all-gather.9.cloned.1.call-start = ((), (), s32[]{:S(2)}) async-start(), calls=%async_computation.2 | async-start | bytes 3342336 | tf_op jit(solution)/shard_map/all_gather | solution.py:78
  9.7 191.8 %all-gather.11.cloned.1.call-start = ((), (), s32[]{:S(2)}) async-start(), calls=%async_computation.4 | async-start | bytes 14483456 | tf_op jit(solution)/shard_map/all_gather | solution.py:44
  13.9 348.5 %all-gather.13.cloned.1.call-start = ((), (), s32[]{:S(2)}) async-start(), calls=%async_computation.5 | async-start | bytes 37748736 | tf_op jit(solution)/shard_map/all_gather | solution.py:15
  111.3 1.8 copy-start.3
  112.3 1.4 copy-start.1
  116.8 4.2 copy-start.6
  129.4 2.6 copy-start.4
  135.0 1.0 copy-start.5
  206.7 0.7 copy-start.8
  206.8 236.2 %reduce-scatter.2.cloned.1.call-start = ((), (), s32[]{:S(2)}) async-start(), calls=%async_computation.3 | async-start | bytes 4718592 | tf_op jit(solution)/shard_map/reduce_scatter | solution.py:131
  376.7 5.6 %copy-start.2 = (bf16[2048,1024]{1,0:T(8,128)(2,1)S(1)}, bf16[2048,1024]{1,0:T(8,128)(2,1)}, u32[]{:S(2)}) copy-start(bf16[2048,1024]{1,0:T(8,128)(2,1)} %reshape_reshape.6) | copy-start | bytes 12582916
  382.3 6.4 %copy-start = (bf16[1024,2048]{1,0:T(8,128)(2,1)}, bf16[1024,2048]{1,0:T(8,128)(2,1)S(1)}, u32[]{:S(2)}) copy-start(bf16[1024,2048]{1,0:T(8,128)(2,1)S(1)} %get-tuple-element.84) | copy-start | bytes 12582916
Sparse Core Ops, SparseCore 0:
  9.7 38.4 all-gather.6
  50.9 53.7 all-gather.8
  106.9 94.6 all-gather.10
  206.9 155.4 all-gather.12
  404.1 38.7 reduce-scatter.1
